TPU v7x, 256 devices: a whole 4x4x8 slice. The times are simulated.
256 devices in a mesh: ctx: 32 (over x, z_lo, core), tp: 8 (over z_hi, y).
Axes of the slice: x: 4, y: 4, z: 8 (z_hi: 2, z_lo: 4; z = z_hi * 4 + z_lo), core: 2. Of those that a mesh axis runs over, the one named last changes fastest.
Arguments:
- queries: bfloat16 [8192, 8192], P('ctx', 'tp'), may hold values from -8 to 8
- key_rows: bfloat16 [8192, 1024], P('ctx', 'tp'), may hold values from -8 to 8
- value_head_rows: bfloat16 [8192, 1024], P('ctx', 'tp'), may hold values from -6 to 6
- ssm_input: bfloat16 [8192, 8192], P('ctx', 'tp'), may hold values from -6 to 6
- gate_input: bfloat16 [8192, 8192], P('ctx', 'tp'), may hold values from -6 to 6
- b_matrix: bfloat16 [8192, 1024], P('ctx', 'tp'), may hold values from -6 to 6
- c_matrix: bfloat16 [8192, 1024], P('ctx', 'tp'), may hold values from -0.5 to 0.5
- step_size: float32 [128, 8192], P('tp', 'ctx'), may hold values from 0.02 to 0.2
- log_decay: float32 [128, 8192], P('tp', 'ctx'), may hold values from -1.5 to 0
- skip_gain: float32 [128], P('tp'), may hold values from 0.5 to 1.5
- norm_gain: bfloat16 [8192], P('tp'), may hold values from 0.099609375 to 1.8984375
Outputs:
- attention_out: bfloat16 [8192, 8192], P('ctx', 'tp')
- mixer_out: bfloat16 [8192, 8192], P('ctx', 'tp')
All inputs are finite; a program needn't handle non-finite values.
Results may differ from a plain program's by a relative error of at most 0.022.
Values may be sent and summed in bfloat16 or wider, within the bound.
No kernel may reach another device: no remote copies, remote signals or barrier semaphores. Data moves between devices by JAX's collectives and lax.ppermute only.
A program may use at most 128 MiB of HBM per device.

v0:
```python
import math
import jax
import jax.numpy as jnp
from jax import lax
from jax.sharding import PartitionSpec as P

HEAD_WIDTH = 128
STATE_HEADS = 128
P_SIZE = 64
N = 128
causal_score = -1e30


def passed_along(block, axis, distance):
    devices = range(lax.axis_size(axis))
    route = [(i - distance, i) for i in devices if i - distance in devices]
    return lax.ppermute(block, axis, route)


def attend_rows(running_in, key_block, value_block, key_start, query_head_rows, query_pos):
    row_count = key_block.shape[0]
    sub_width = math.gcd(row_count, 512)
    kv_heads = query_head_rows.shape[1]
    score_factor = query_head_rows.shape[3] ** (-0.5)

    def sub_step(sub_id, running):
        run_max, run_sum, summed_so_far = running
        offset = sub_id * sub_width
        key_portion = key_block.reshape(sub_width, kv_heads, -1)
        value_portion = value_block.reshape(sub_width, kv_heads, -1)
        key_pos = key_start + offset + jnp.arange(sub_width, dtype=jnp.int32)
        is_valid = key_pos[None, :] <= query_pos[:, None]
        score_matrix = (
            jnp.einsum(
                "faqo,bao->aqfb", query_head_rows, key_portion, preferred_element_type=jnp.float32
            )
            * score_factor
        )
        score_matrix = jnp.where(is_valid, score_matrix, causal_score)
        new_max = jnp.maximum(run_max, jnp.max(score_matrix, axis=-1))
        weights = jnp.where(is_valid, jnp.exp(score_matrix - new_max[..., None]), 0.0)
        correction_factor = jnp.exp(run_max - new_max)
        run_sum = run_sum * correction_factor + jnp.sum(weights, axis=-1)
        summed_so_far = summed_so_far * correction_factor[..., None] + jnp.einsum(
            "wlhc,cwm->wlhm",
            weights.astype(jnp.bfloat16),
            value_portion,
            preferred_element_type=jnp.float32,
        )
        return (new_max, run_sum, summed_so_far)

    return lax.fori_loop(0, row_count // sub_width, sub_step, running_in)


def local(
    queries,
    key_rows,
    value_head_rows,
    ssm_input,
    gate_input,
    b_matrix,
    c_matrix,
    step_size,
    log_decay,
    skip_gain,
    norm_gain,
):
    tok_rows = queries.shape[0]
    kv_heads = key_rows.shape[1] // HEAD_WIDTH
    query_per_key_heads = queries.shape[1] // HEAD_WIDTH // kv_heads
    query_head_rows = queries.reshape(tok_rows, kv_heads, query_per_key_heads, HEAD_WIDTH)
    ctx_count = lax.axis_size("ctx")
    position = lax.axis_index("ctx")
    query_pos = position * tok_rows + jnp.arange(tok_rows, dtype=jnp.int32)
    starting_state = (
        jnp.full((kv_heads, query_per_key_heads, tok_rows), causal_score, jnp.float32),
        jnp.zeros((kv_heads, query_per_key_heads, tok_rows), jnp.float32),
        jnp.zeros((kv_heads, query_per_key_heads, tok_rows, HEAD_WIDTH), jnp.float32),
    )
    first_pass = attend_rows(
        starting_state, key_rows, value_head_rows, position * tok_rows, query_head_rows, query_pos
    )

    def cycle_step(step_id, state):
        stacked, running = state
        stacked = passed_along(stacked, "ctx", 1)
        sender_index = position - step_id
        key_start = jnp.where(sender_index >= 0, sender_index * tok_rows, ctx_count * tok_rows)
        return (
            stacked,
            attend_rows(running, stacked[0], stacked[1], key_start, query_head_rows, query_pos),
        )

    _, (run_max, run_sum, summed_so_far) = lax.fori_loop(
        1, ctx_count, cycle_step, (jnp.stack((key_rows, value_head_rows)), first_pass)
    )
    attention_out = (
        (summed_so_far / run_sum[..., None])
        .transpose(2, 0, 1, 3)
        .reshape(tok_rows, -1)
        .astype(jnp.bfloat16)
    )
    heads_local = step_size.shape[0]
    groups_local = b_matrix.shape[1] // N
    heads_group = heads_local // groups_local
    mixer_in = ssm_input.reshape(tok_rows, groups_local, heads_group, P_SIZE)
    in_maps = b_matrix.reshape(tok_rows, groups_local, N)
    out_maps = c_matrix.reshape(tok_rows, groups_local, N)
    steps_here = step_size.reshape(groups_local, heads_group, tok_rows)
    cumul = jnp.cumsum(log_decay.reshape(groups_local, heads_group, tok_rows), axis=-1)
    causal = jnp.tril(jnp.ones((tok_rows, tok_rows), dtype=bool))
    gram = jnp.einsum("tgn,sgn->gts", out_maps, in_maps, preferred_element_type=jnp.float32)
    spread = jnp.where(causal, cumul[..., :, None] - cumul[..., None, :], 0.0)
    mixing = jnp.where(
        causal, gram[:, None] * jnp.exp(spread) * steps_here[..., None, :], 0.0
    ).astype(jnp.bfloat16)
    inner = jnp.einsum("ghts,sghp->tghp", mixing, mixer_in, preferred_element_type=jnp.float32)
    weight_end = jnp.exp(cumul[..., -1:] - cumul) * steps_here
    weighted = (mixer_in * weight_end.transpose(2, 0, 1)[..., None]).astype(jnp.bfloat16)
    local_state = jnp.einsum(
        "sghp,sgn->ghpn", weighted, in_maps, preferred_element_type=jnp.float32
    )
    block_decay = jnp.exp(cumul[..., -1])

    def relay_step(step_id, pair):
        received, outgoing = pair
        received = passed_along(outgoing.astype(jnp.bfloat16), "ctx", 1).astype(outgoing.dtype)
        return (received, block_decay[..., None, None] * received + local_state)

    incoming, _ = lax.fori_loop(
        1, ctx_count, relay_step, (jnp.zeros_like(local_state), local_state)
    )
    carried_out = jnp.einsum(
        "ghpn,tgn->tghp", incoming, out_maps.astype(jnp.float32), precision=lax.Precision.HIGHEST
    )
    carried_out = carried_out * jnp.exp(cumul).transpose(2, 0, 1)[..., None]
    direct = skip_gain.reshape(groups_local, heads_group)[None, :, :, None] * mixer_in.astype(
        jnp.float32
    )
    outputs = (inner + carried_out + direct).reshape(tok_rows, -1)
    gated = outputs * jax.nn.silu(gate_input.astype(jnp.float32))
    square_total = lax.psum(jnp.sum(gated * gated, axis=-1), "tp")
    scaling = lax.rsqrt(square_total / (STATE_HEADS * P_SIZE) + 1e-05)
    mixer_out = (gated * scaling[:, None] * norm_gain.astype(jnp.float32)).astype(jnp.bfloat16)
    return (attention_out, mixer_out)


def solution(mesh):
    placed = (
        P("ctx", "tp"),
        P("ctx", "tp"),
        P("ctx", "tp"),
        P("ctx", "tp"),
        P("ctx", "tp"),
        P("ctx", "tp"),
        P("ctx", "tp"),
        P("tp", "ctx"),
        P("tp", "ctx"),
        P("tp"),
        P("tp"),
    )
    return jax.shard_map(
        local,
        mesh=mesh,
        in_specs=placed,
        out_specs=(P("ctx", "tp"), P("ctx", "tp")),
        check_vma=False,
    )
```

profile of v0, /device:TPU:2, one launch (start us, length us, event | category | flops | bytes accessed | tf_op | source)
XLA Modules:
  0.0 740.2 jit_solution(10609625799831482986)
XLA Ops:
  5.4 343.8 %while.55 = (s32[]{:T(128)}, bf16[2,256,128]{2,1,0:T(8,128)(2,1)S(1)}, f32[1,8,256]{2,1,0:T(8,128)S(1)}, f32[1,8,256]{2,1,0:T(8,128)S(1)}, f32[1,8,256,128]{3,2,...) while((s32[]{:T(128)}, ...), condition=%wide.region_5.6_spmd.clone, body=%wide.region_2.5_spmd.clone.sunk | while | flops 275847680 | bytes 10227923 | solution.py:94
  353.0 347.9 %while.54 = (s32[]{:T(128)}, f32[1,16,64,128]{3,2,1,0:T(8,128)}, bf16[1,16,64,128]{3,2,1,0:T(8,128)(2,1)S(1)}, f32[1,16]{1,0:T(1,128)S(1)}, f32[1,16,64,128]{3,2,1,0:T(8,128)S(1)}, /*index=5*/s32[]{:T(128)}) while((s32[]{:T(128)}, f32[1,16,64,128]{3,2,1,0:T(8,128)}, bf16[1,16,64,128]{3,2,1,0:T(8,128)(2,1)S(1)}, f32[1,16]{1,0:T(1,128)S(1)}, ...), condition=%wide.region_9.10_spmd, body=%wide.region_8.9_spmd.sunk | while | flops 524290 | bytes 2621613 | solution.py:130
  366.1 8.5 %collective-permute-done = bf16[1,16,64,128]{3,2,1,0:T(8,128)(2,1)S(1)} collective-permute-done((bf16[1,16,64,128]{3,2,1,0:T(8,128)(2,1)S(1)}, bf16[1,16,64,128]{3,2,1,0:T(8,128)(2,1)S(1)}, u32[]{:S(2)}, u32[]{:S(2)}) %collective-permute-start) | collective-permute-done | bytes 262176 | tf_op jit(solution)/shard_map/while/body/eval_jaxpr/ppermute | solution.py:17
  377.4 8.5 %collective-permute-done = bf16[1,16,64,128]{3,2,1,0:T(8,128)(2,1)S(1)} collective-permute-done((bf16[1,16,64,128]{3,2,1,0:T(8,128)(2,1)S(1)}, bf16[1,16,64,128]{3,2,1,0:T(8,128)(2,1)S(1)}, u32[]{:S(2)}, u32[]{:S(2)}) %collective-permute-start) | collective-permute-done | bytes 262176 | tf_op jit(solution)/shard_map/while/body/eval_jaxpr/ppermute | solution.py:17
  399.8 8.5 %collective-permute-done = bf16[1,16,64,128]{3,2,1,0:T(8,128)(2,1)S(1)} collective-permute-done((bf16[1,16,64,128]{3,2,1,0:T(8,128)(2,1)S(1)}, bf16[1,16,64,128]{3,2,1,0:T(8,128)(2,1)S(1)}, u32[]{:S(2)}, u32[]{:S(2)}) %collective-permute-start) | collective-permute-done | bytes 262176 | tf_op jit(solution)/shard_map/while/body/eval_jaxpr/ppermute | solution.py:17
  411.0 8.5 %collective-permute-done = bf16[1,16,64,128]{3,2,1,0:T(8,128)(2,1)S(1)} collective-permute-done((bf16[1,16,64,128]{3,2,1,0:T(8,128)(2,1)S(1)}, bf16[1,16,64,128]{3,2,1,0:T(8,128)(2,1)S(1)}, u32[]{:S(2)}, u32[]{:S(2)}) %collective-permute-start) | collective-permute-done | bytes 262176 | tf_op jit(solution)/shard_map/while/body/eval_jaxpr/ppermute | solution.py:17
  433.4 8.5 %collective-permute-done = bf16[1,16,64,128]{3,2,1,0:T(8,128)(2,1)S(1)} collective-permute-done((bf16[1,16,64,128]{3,2,1,0:T(8,128)(2,1)S(1)}, bf16[1,16,64,128]{3,2,1,0:T(8,128)(2,1)S(1)}, u32[]{:S(2)}, u32[]{:S(2)}) %collective-permute-start) | collective-permute-done | bytes 262176 | tf_op jit(solution)/shard_map/while/body/eval_jaxpr/ppermute | solution.py:17
  444.7 8.5 %collective-permute-done = bf16[1,16,64,128]{3,2,1,0:T(8,128)(2,1)S(1)} collective-permute-done((bf16[1,16,64,128]{3,2,1,0:T(8,128)(2,1)S(1)}, bf16[1,16,64,128]{3,2,1,0:T(8,128)(2,1)S(1)}, u32[]{:S(2)}, u32[]{:S(2)}) %collective-permute-start) | collective-permute-done | bytes 262176 | tf_op jit(solution)/shard_map/while/body/eval_jaxpr/ppermute | solution.py:17
  455.9 8.5 %collective-permute-done = bf16[1,16,64,128]{3,2,1,0:T(8,128)(2,1)S(1)} collective-permute-done((bf16[1,16,64,128]{3,2,1,0:T(8,128)(2,1)S(1)}, bf16[1,16,64,128]{3,2,1,0:T(8,128)(2,1)S(1)}, u32[]{:S(2)}, u32[]{:S(2)}) %collective-permute-start) | collective-permute-done | bytes 262176 | tf_op jit(solution)/shard_map/while/body/eval_jaxpr/ppermute | solution.py:17
  478.3 8.5 %collective-permute-done = bf16[1,16,64,128]{3,2,1,0:T(8,128)(2,1)S(1)} collective-permute-done((bf16[1,16,64,128]{3,2,1,0:T(8,128)(2,1)S(1)}, bf16[1,16,64,128]{3,2,1,0:T(8,128)(2,1)S(1)}, u32[]{:S(2)}, u32[]{:S(2)}) %collective-permute-start) | collective-permute-done | bytes 262176 | tf_op jit(solution)/shard_map/while/body/eval_jaxpr/ppermute | solution.py:17
  489.5 8.5 %collective-permute-done = bf16[1,16,64,128]{3,2,1,0:T(8,128)(2,1)S(1)} collective-permute-done((bf16[1,16,64,128]{3,2,1,0:T(8,128)(2,1)S(1)}, bf16[1,16,64,128]{3,2,1,0:T(8,128)(2,1)S(1)}, u32[]{:S(2)}, u32[]{:S(2)}) %collective-permute-start) | collective-permute-done | bytes 262176 | tf_op jit(solution)/shard_map/while/body/eval_jaxpr/ppermute | solution.py:17
  512.0 8.5 %collective-permute-done = bf16[1,16,64,128]{3,2,1,0:T(8,128)(2,1)S(1)} collective-permute-done((bf16[1,16,64,128]{3,2,1,0:T(8,128)(2,1)S(1)}, bf16[1,16,64,128]{3,2,1,0:T(8,128)(2,1)S(1)}, u32[]{:S(2)}, u32[]{:S(2)}) %collective-permute-start) | collective-permute-done | bytes 262176 | tf_op jit(solution)/shard_map/while/body/eval_jaxpr/ppermute | solution.py:17
  523.2 8.5 %collective-permute-done = bf16[1,16,64,128]{3,2,1,0:T(8,128)(2,1)S(1)} collective-permute-done((bf16[1,16,64,128]{3,2,1,0:T(8,128)(2,1)S(1)}, bf16[1,16,64,128]{3,2,1,0:T(8,128)(2,1)S(1)}, u32[]{:S(2)}, u32[]{:S(2)}) %collective-permute-start) | collective-permute-done | bytes 262176 | tf_op jit(solution)/shard_map/while/body/eval_jaxpr/ppermute | solution.py:17
  545.6 8.5 %collective-permute-done = bf16[1,16,64,128]{3,2,1,0:T(8,128)(2,1)S(1)} collective-permute-done((bf16[1,16,64,128]{3,2,1,0:T(8,128)(2,1)S(1)}, bf16[1,16,64,128]{3,2,1,0:T(8,128)(2,1)S(1)}, u32[]{:S(2)}, u32[]{:S(2)}) %collective-permute-start) | collective-permute-done | bytes 262176 | tf_op jit(solution)/shard_map/while/body/eval_jaxpr/ppermute | solution.py:17
  556.9 8.5 %collective-permute-done = bf16[1,16,64,128]{3,2,1,0:T(8,128)(2,1)S(1)} collective-permute-done((bf16[1,16,64,128]{3,2,1,0:T(8,128)(2,1)S(1)}, bf16[1,16,64,128]{3,2,1,0:T(8,128)(2,1)S(1)}, u32[]{:S(2)}, u32[]{:S(2)}) %collective-permute-start) | collective-permute-done | bytes 262176 | tf_op jit(solution)/shard_map/while/body/eval_jaxpr/ppermute | solution.py:17
  579.3 8.5 %collective-permute-done = bf16[1,16,64,128]{3,2,1,0:T(8,128)(2,1)S(1)} collective-permute-done((bf16[1,16,64,128]{3,2,1,0:T(8,128)(2,1)S(1)}, bf16[1,16,64,128]{3,2,1,0:T(8,128)(2,1)S(1)}, u32[]{:S(2)}, u32[]{:S(2)}) %collective-permute-start) | collective-permute-done | bytes 262176 | tf_op jit(solution)/shard_map/while/body/eval_jaxpr/ppermute | solution.py:17
  590.5 8.5 %collective-permute-done = bf16[1,16,64,128]{3,2,1,0:T(8,128)(2,1)S(1)} collective-permute-done((bf16[1,16,64,128]{3,2,1,0:T(8,128)(2,1)S(1)}, bf16[1,16,64,128]{3,2,1,0:T(8,128)(2,1)S(1)}, u32[]{:S(2)}, u32[]{:S(2)}) %collective-permute-start) | collective-permute-done | bytes 262176 | tf_op jit(solution)/shard_map/while/body/eval_jaxpr/ppermute | solution.py:17
  613.0 8.5 %collective-permute-done = bf16[1,16,64,128]{3,2,1,0:T(8,128)(2,1)S(1)} collective-permute-done((bf16[1,16,64,128]{3,2,1,0:T(8,128)(2,1)S(1)}, bf16[1,16,64,128]{3,2,1,0:T(8,128)(2,1)S(1)}, u32[]{:S(2)}, u32[]{:S(2)}) %collective-permute-start) | collective-permute-done | bytes 262176 | tf_op jit(solution)/shard_map/while/body/eval_jaxpr/ppermute | solution.py:17
  624.2 8.5 %collective-permute-done = bf16[1,16,64,128]{3,2,1,0:T(8,128)(2,1)S(1)} collective-permute-done((bf16[1,16,64,128]{3,2,1,0:T(8,128)(2,1)S(1)}, bf16[1,16,64,128]{3,2,1,0:T(8,128)(2,1)S(1)}, u32[]{:S(2)}, u32[]{:S(2)}) %collective-permute-start) | collective-permute-done | bytes 262176 | tf_op jit(solution)/shard_map/while/body/eval_jaxpr/ppermute | solution.py:17
  646.6 8.5 %collective-permute-done = bf16[1,16,64,128]{3,2,1,0:T(8,128)(2,1)S(1)} collective-permute-done((bf16[1,16,64,128]{3,2,1,0:T(8,128)(2,1)S(1)}, bf16[1,16,64,128]{3,2,1,0:T(8,128)(2,1)S(1)}, u32[]{:S(2)}, u32[]{:S(2)}) %collective-permute-start) | collective-permute-done | bytes 262176 | tf_op jit(solution)/shard_map/while/body/eval_jaxpr/ppermute | solution.py:17
  657.8 8.5 %collective-permute-done = bf16[1,16,64,128]{3,2,1,0:T(8,128)(2,1)S(1)} collective-permute-done((bf16[1,16,64,128]{3,2,1,0:T(8,128)(2,1)S(1)}, bf16[1,16,64,128]{3,2,1,0:T(8,128)(2,1)S(1)}, u32[]{:S(2)}, u32[]{:S(2)}) %collective-permute-start) | collective-permute-done | bytes 262176 | tf_op jit(solution)/shard_map/while/body/eval_jaxpr/ppermute | solution.py:17
  680.3 8.5 %collective-permute-done = bf16[1,16,64,128]{3,2,1,0:T(8,128)(2,1)S(1)} collective-permute-done((bf16[1,16,64,128]{3,2,1,0:T(8,128)(2,1)S(1)}, bf16[1,16,64,128]{3,2,1,0:T(8,128)(2,1)S(1)}, u32[]{:S(2)}, u32[]{:S(2)}) %collective-permute-start) | collective-permute-done | bytes 262176 | tf_op jit(solution)/shard_map/while/body/eval_jaxpr/ppermute | solution.py:17
  691.5 8.5 %collective-permute-done = bf16[1,16,64,128]{3,2,1,0:T(8,128)(2,1)S(1)} collective-permute-done((bf16[1,16,64,128]{3,2,1,0:T(8,128)(2,1)S(1)}, bf16[1,16,64,128]{3,2,1,0:T(8,128)(2,1)S(1)}, u32[]{:S(2)}, u32[]{:S(2)}) %collective-permute-start) | collective-permute-done | bytes 262176 | tf_op jit(solution)/shard_map/while/body/eval_jaxpr/ppermute | solution.py:17
  705.6 33.4 %psum.7 = f32[256]{0:T(256)S(1)} all-reduce(f32[256]{0:T(256)S(1)} %multiply_reduce_fusion), channel_id=1, replica_groups=mesh['ctx'=32,'tp'=8] {'tp'}, use_global_device_ids=true, to_apply=%region_11.12 | all-reduce | flops 256 | bytes 2048 | tf_op jit(solution)/shard_map/psum | solution.py:142
  (473 shorter events, 524.9 us)
Async XLA Ops:
  353.0 10.4 %collective-permute-start = (bf16[1,16,64,128]{3,2,1,0:T(8,128)(2,1)S(1)}, bf16[1,16,64,128]{3,2,1,0:T(8,128)(2,1)S(1)}, u32[]{:S(2)}, u32[]{:S(2)}) collective-permute-start(bf16[1,16,64,128]{3,2,1,0:T(8,128)(2,1)S(1)} %get-tuple-element.471), channel_id=1, source_target_pairs={{0,8},{8,16},{16,24},{24,32},{32,40},{40,48},{48,56},{56,64},{64,7... | collective-permute-start | bytes 786440 | tf_op jit(solution)/shard_map/while/body/eval_jaxpr/ppermute | solution.py:17
  364.2 10.4 %collective-permute-start = (bf16[1,16,64,128]{3,2,1,0:T(8,128)(2,1)S(1)}, bf16[1,16,64,128]{3,2,1,0:T(8,128)(2,1)S(1)}, u32[]{:S(2)}, u32[]{:S(2)}) collective-permute-start(bf16[1,16,64,128]{3,2,1,0:T(8,128)(2,1)S(1)} %get-tuple-element.471), channel_id=1, source_target_pairs={{0,8},{8,16},{16,24},{24,32},{32,40},{40,48},{48,56},{56,64},{64,7... | collective-permute-start | bytes 786440 | tf_op jit(solution)/shard_map/while/body/eval_jaxpr/ppermute | solution.py:17
  375.4 10.4 %collective-permute-start = (bf16[1,16,64,128]{3,2,1,0:T(8,128)(2,1)S(1)}, bf16[1,16,64,128]{3,2,1,0:T(8,128)(2,1)S(1)}, u32[]{:S(2)}, u32[]{:S(2)}) collective-permute-start(bf16[1,16,64,128]{3,2,1,0:T(8,128)(2,1)S(1)} %get-tuple-element.471), channel_id=1, source_target_pairs={{0,8},{8,16},{16,24},{24,32},{32,40},{40,48},{48,56},{56,64},{64,7... | collective-permute-start | bytes 786440 | tf_op jit(solution)/shard_map/while/body/eval_jaxpr/ppermute | solution.py:17
  386.7 10.4 %collective-permute-start = (bf16[1,16,64,128]{3,2,1,0:T(8,128)(2,1)S(1)}, bf16[1,16,64,128]{3,2,1,0:T(8,128)(2,1)S(1)}, u32[]{:S(2)}, u32[]{:S(2)}) collective-permute-start(bf16[1,16,64,128]{3,2,1,0:T(8,128)(2,1)S(1)} %get-tuple-element.471), channel_id=1, source_target_pairs={{0,8},{8,16},{16,24},{24,32},{32,40},{40,48},{48,56},{56,64},{64,7... | collective-permute-start | bytes 786440 | tf_op jit(solution)/shard_map/while/body/eval_jaxpr/ppermute | solution.py:17
  397.9 10.4 %collective-permute-start = (bf16[1,16,64,128]{3,2,1,0:T(8,128)(2,1)S(1)}, bf16[1,16,64,128]{3,2,1,0:T(8,128)(2,1)S(1)}, u32[]{:S(2)}, u32[]{:S(2)}) collective-permute-start(bf16[1,16,64,128]{3,2,1,0:T(8,128)(2,1)S(1)} %get-tuple-element.471), channel_id=1, source_target_pairs={{0,8},{8,16},{16,24},{24,32},{32,40},{40,48},{48,56},{56,64},{64,7... | collective-permute-start | bytes 786440 | tf_op jit(solution)/shard_map/while/body/eval_jaxpr/ppermute | solution.py:17
  409.1 10.4 %collective-permute-start = (bf16[1,16,64,128]{3,2,1,0:T(8,128)(2,1)S(1)}, bf16[1,16,64,128]{3,2,1,0:T(8,128)(2,1)S(1)}, u32[]{:S(2)}, u32[]{:S(2)}) collective-permute-start(bf16[1,16,64,128]{3,2,1,0:T(8,128)(2,1)S(1)} %get-tuple-element.471), channel_id=1, source_target_pairs={{0,8},{8,16},{16,24},{24,32},{32,40},{40,48},{48,56},{56,64},{64,7... | collective-permute-start | bytes 786440 | tf_op jit(solution)/shard_map/while/body/eval_jaxpr/ppermute | solution.py:17
  420.3 10.4 %collective-permute-start = (bf16[1,16,64,128]{3,2,1,0:T(8,128)(2,1)S(1)}, bf16[1,16,64,128]{3,2,1,0:T(8,128)(2,1)S(1)}, u32[]{:S(2)}, u32[]{:S(2)}) collective-permute-start(bf16[1,16,64,128]{3,2,1,0:T(8,128)(2,1)S(1)} %get-tuple-element.471), channel_id=1, source_target_pairs={{0,8},{8,16},{16,24},{24,32},{32,40},{40,48},{48,56},{56,64},{64,7... | collective-permute-start | bytes 786440 | tf_op jit(solution)/shard_map/while/body/eval_jaxpr/ppermute | solution.py:17
  431.5 10.4 %collective-permute-start = (bf16[1,16,64,128]{3,2,1,0:T(8,128)(2,1)S(1)}, bf16[1,16,64,128]{3,2,1,0:T(8,128)(2,1)S(1)}, u32[]{:S(2)}, u32[]{:S(2)}) collective-permute-start(bf16[1,16,64,128]{3,2,1,0:T(8,128)(2,1)S(1)} %get-tuple-element.471), channel_id=1, source_target_pairs={{0,8},{8,16},{16,24},{24,32},{32,40},{40,48},{48,56},{56,64},{64,7... | collective-permute-start | bytes 786440 | tf_op jit(solution)/shard_map/while/body/eval_jaxpr/ppermute | solution.py:17
  442.8 10.4 %collective-permute-start = (bf16[1,16,64,128]{3,2,1,0:T(8,128)(2,1)S(1)}, bf16[1,16,64,128]{3,2,1,0:T(8,128)(2,1)S(1)}, u32[]{:S(2)}, u32[]{:S(2)}) collective-permute-start(bf16[1,16,64,128]{3,2,1,0:T(8,128)(2,1)S(1)} %get-tuple-element.471), channel_id=1, source_target_pairs={{0,8},{8,16},{16,24},{24,32},{32,40},{40,48},{48,56},{56,64},{64,7... | collective-permute-start | bytes 786440 | tf_op jit(solution)/shard_map/while/body/eval_jaxpr/ppermute | solution.py:17
  454.0 10.4 %collective-permute-start = (bf16[1,16,64,128]{3,2,1,0:T(8,128)(2,1)S(1)}, bf16[1,16,64,128]{3,2,1,0:T(8,128)(2,1)S(1)}, u32[]{:S(2)}, u32[]{:S(2)}) collective-permute-start(bf16[1,16,64,128]{3,2,1,0:T(8,128)(2,1)S(1)} %get-tuple-element.471), channel_id=1, source_target_pairs={{0,8},{8,16},{16,24},{24,32},{32,40},{40,48},{48,56},{56,64},{64,7... | collective-permute-start | bytes 786440 | tf_op jit(solution)/shard_map/while/body/eval_jaxpr/ppermute | solution.py:17
  465.2 10.4 %collective-permute-start = (bf16[1,16,64,128]{3,2,1,0:T(8,128)(2,1)S(1)}, bf16[1,16,64,128]{3,2,1,0:T(8,128)(2,1)S(1)}, u32[]{:S(2)}, u32[]{:S(2)}) collective-permute-start(bf16[1,16,64,128]{3,2,1,0:T(8,128)(2,1)S(1)} %get-tuple-element.471), channel_id=1, source_target_pairs={{0,8},{8,16},{16,24},{24,32},{32,40},{40,48},{48,56},{56,64},{64,7... | collective-permute-start | bytes 786440 | tf_op jit(solution)/shard_map/while/body/eval_jaxpr/ppermute | solution.py:17
  476.4 10.4 %collective-permute-start = (bf16[1,16,64,128]{3,2,1,0:T(8,128)(2,1)S(1)}, bf16[1,16,64,128]{3,2,1,0:T(8,128)(2,1)S(1)}, u32[]{:S(2)}, u32[]{:S(2)}) collective-permute-start(bf16[1,16,64,128]{3,2,1,0:T(8,128)(2,1)S(1)} %get-tuple-element.471), channel_id=1, source_target_pairs={{0,8},{8,16},{16,24},{24,32},{32,40},{40,48},{48,56},{56,64},{64,7... | collective-permute-start | bytes 786440 | tf_op jit(solution)/shard_map/while/body/eval_jaxpr/ppermute | solution.py:17
  487.6 10.4 %collective-permute-start = (bf16[1,16,64,128]{3,2,1,0:T(8,128)(2,1)S(1)}, bf16[1,16,64,128]{3,2,1,0:T(8,128)(2,1)S(1)}, u32[]{:S(2)}, u32[]{:S(2)}) collective-permute-start(bf16[1,16,64,128]{3,2,1,0:T(8,128)(2,1)S(1)} %get-tuple-element.471), channel_id=1, source_target_pairs={{0,8},{8,16},{16,24},{24,32},{32,40},{40,48},{48,56},{56,64},{64,7... | collective-permute-start | bytes 786440 | tf_op jit(solution)/shard_map/while/body/eval_jaxpr/ppermute | solution.py:17
  498.8 10.4 %collective-permute-start = (bf16[1,16,64,128]{3,2,1,0:T(8,128)(2,1)S(1)}, bf16[1,16,64,128]{3,2,1,0:T(8,128)(2,1)S(1)}, u32[]{:S(2)}, u32[]{:S(2)}) collective-permute-start(bf16[1,16,64,128]{3,2,1,0:T(8,128)(2,1)S(1)} %get-tuple-element.471), channel_id=1, source_target_pairs={{0,8},{8,16},{16,24},{24,32},{32,40},{40,48},{48,56},{56,64},{64,7... | collective-permute-start | bytes 786440 | tf_op jit(solution)/shard_map/while/body/eval_jaxpr/ppermute | solution.py:17
  510.1 10.4 %collective-permute-start = (bf16[1,16,64,128]{3,2,1,0:T(8,128)(2,1)S(1)}, bf16[1,16,64,128]{3,2,1,0:T(8,128)(2,1)S(1)}, u32[]{:S(2)}, u32[]{:S(2)}) collective-permute-start(bf16[1,16,64,128]{3,2,1,0:T(8,128)(2,1)S(1)} %get-tuple-element.471), channel_id=1, source_target_pairs={{0,8},{8,16},{16,24},{24,32},{32,40},{40,48},{48,56},{56,64},{64,7... | collective-permute-start | bytes 786440 | tf_op jit(solution)/shard_map/while/body/eval_jaxpr/ppermute | solution.py:17
  521.3 10.4 %collective-permute-start = (bf16[1,16,64,128]{3,2,1,0:T(8,128)(2,1)S(1)}, bf16[1,16,64,128]{3,2,1,0:T(8,128)(2,1)S(1)}, u32[]{:S(2)}, u32[]{:S(2)}) collective-permute-start(bf16[1,16,64,128]{3,2,1,0:T(8,128)(2,1)S(1)} %get-tuple-element.471), channel_id=1, source_target_pairs={{0,8},{8,16},{16,24},{24,32},{32,40},{40,48},{48,56},{56,64},{64,7... | collective-permute-start | bytes 786440 | tf_op jit(solution)/shard_map/while/body/eval_jaxpr/ppermute | solution.py:17
  532.5 10.4 %collective-permute-start = (bf16[1,16,64,128]{3,2,1,0:T(8,128)(2,1)S(1)}, bf16[1,16,64,128]{3,2,1,0:T(8,128)(2,1)S(1)}, u32[]{:S(2)}, u32[]{:S(2)}) collective-permute-start(bf16[1,16,64,128]{3,2,1,0:T(8,128)(2,1)S(1)} %get-tuple-element.471), channel_id=1, source_target_pairs={{0,8},{8,16},{16,24},{24,32},{32,40},{40,48},{48,56},{56,64},{64,7... | collective-permute-start | bytes 786440 | tf_op jit(solution)/shard_map/while/body/eval_jaxpr/ppermute | solution.py:17
  554.9 10.4 %collective-permute-start = (bf16[1,16,64,128]{3,2,1,0:T(8,128)(2,1)S(1)}, bf16[1,16,64,128]{3,2,1,0:T(8,128)(2,1)S(1)}, u32[]{:S(2)}, u32[]{:S(2)}) collective-permute-start(bf16[1,16,64,128]{3,2,1,0:T(8,128)(2,1)S(1)} %get-tuple-element.471), channel_id=1, source_target_pairs={{0,8},{8,16},{16,24},{24,32},{32,40},{40,48},{48,56},{56,64},{64,7... | collective-permute-start | bytes 786440 | tf_op jit(solution)/shard_map/while/body/eval_jaxpr/ppermute | solution.py:17
  588.6 10.4 %collective-permute-start = (bf16[1,16,64,128]{3,2,1,0:T(8,128)(2,1)S(1)}, bf16[1,16,64,128]{3,2,1,0:T(8,128)(2,1)S(1)}, u32[]{:S(2)}, u32[]{:S(2)}) collective-permute-start(bf16[1,16,64,128]{3,2,1,0:T(8,128)(2,1)S(1)} %get-tuple-element.471), channel_id=1, source_target_pairs={{0,8},{8,16},{16,24},{24,32},{32,40},{40,48},{48,56},{56,64},{64,7... | collective-permute-start | bytes 786440 | tf_op jit(solution)/shard_map/while/body/eval_jaxpr/ppermute | solution.py:17
  622.3 10.4 %collective-permute-start = (bf16[1,16,64,128]{3,2,1,0:T(8,128)(2,1)S(1)}, bf16[1,16,64,128]{3,2,1,0:T(8,128)(2,1)S(1)}, u32[]{:S(2)}, u32[]{:S(2)}) collective-permute-start(bf16[1,16,64,128]{3,2,1,0:T(8,128)(2,1)S(1)} %get-tuple-element.471), channel_id=1, source_target_pairs={{0,8},{8,16},{16,24},{24,32},{32,40},{40,48},{48,56},{56,64},{64,7... | collective-permute-start | bytes 786440 | tf_op jit(solution)/shard_map/while/body/eval_jaxpr/ppermute | solution.py:17
  655.9 10.4 %collective-permute-start = (bf16[1,16,64,128]{3,2,1,0:T(8,128)(2,1)S(1)}, bf16[1,16,64,128]{3,2,1,0:T(8,128)(2,1)S(1)}, u32[]{:S(2)}, u32[]{:S(2)}) collective-permute-start(bf16[1,16,64,128]{3,2,1,0:T(8,128)(2,1)S(1)} %get-tuple-element.471), channel_id=1, source_target_pairs={{0,8},{8,16},{16,24},{24,32},{32,40},{40,48},{48,56},{56,64},{64,7... | collective-permute-start | bytes 786440 | tf_op jit(solution)/shard_map/while/body/eval_jaxpr/ppermute | solution.py:17
  667.1 10.4 %collective-permute-start = (bf16[1,16,64,128]{3,2,1,0:T(8,128)(2,1)S(1)}, bf16[1,16,64,128]{3,2,1,0:T(8,128)(2,1)S(1)}, u32[]{:S(2)}, u32[]{:S(2)}) collective-permute-start(bf16[1,16,64,128]{3,2,1,0:T(8,128)(2,1)S(1)} %get-tuple-element.471), channel_id=1, source_target_pairs={{0,8},{8,16},{16,24},{24,32},{32,40},{40,48},{48,56},{56,64},{64,7... | collective-permute-start | bytes 786440 | tf_op jit(solution)/shard_map/while/body/eval_jaxpr/ppermute | solution.py:17
  678.4 10.4 %collective-permute-start = (bf16[1,16,64,128]{3,2,1,0:T(8,128)(2,1)S(1)}, bf16[1,16,64,128]{3,2,1,0:T(8,128)(2,1)S(1)}, u32[]{:S(2)}, u32[]{:S(2)}) collective-permute-start(bf16[1,16,64,128]{3,2,1,0:T(8,128)(2,1)S(1)} %get-tuple-element.471), channel_id=1, source_target_pairs={{0,8},{8,16},{16,24},{24,32},{32,40},{40,48},{48,56},{56,64},{64,7... | collective-permute-start | bytes 786440 | tf_op jit(solution)/shard_map/while/body/eval_jaxpr/ppermute | solution.py:17
  689.6 10.4 %collective-permute-start = (bf16[1,16,64,128]{3,2,1,0:T(8,128)(2,1)S(1)}, bf16[1,16,64,128]{3,2,1,0:T(8,128)(2,1)S(1)}, u32[]{:S(2)}, u32[]{:S(2)}) collective-permute-start(bf16[1,16,64,128]{3,2,1,0:T(8,128)(2,1)S(1)} %get-tuple-element.471), channel_id=1, source_target_pairs={{0,8},{8,16},{16,24},{24,32},{32,40},{40,48},{48,56},{56,64},{64,7... | collective-permute-start | bytes 786440 | tf_op jit(solution)/shard_map/while/body/eval_jaxpr/ppermute | solution.py:17
  (48 other events, 1066.6 us)
where the time goes:
time: 743 us; the launch traced here: 740 us
  waiting for transfers between devices  477 us (64%)
  starting transfers between devices  119 us (16%)
  matrix products  52.5 us (7%)
  other arithmetic  50.4 us (7%)
  blocking collectives  33.4 us (4%)
    ppermute x62, waiting for transfers between devices, passed_along(): return lax.ppermute(block, axis, route)  477 us
    ppermute x62, starting transfers between devices, passed_along(): return lax.ppermute(block, axis, route)  119 us
    psum x1, blocking collectives, local(): square_total = lax.psum(jnp.sum(gated * gated, axis=-1), 'tp')  33.4 us
    dot_general x32, matrix products, sub_step(): jnp.einsum('wlhc,cwm->wlhm', weights.astype(jnp.bfloat16), value_portion,...  33 us
    add x31, other arithmetic, relay_step(): return (received, block_decay[..., None, None] * received + local_state)  26.1 us
    reduce_sum x32, other arithmetic, sub_step(): run_sum = run_sum * correction_factor + jnp.sum(weights, axis=-1)  16.5 us
    dot_general x32, matrix products, sub_step(): jnp.einsum('faqo,bao->aqfb', query_head_rows, key_portion, preferred_elem...  15.9 us
  transfers between devices with their start and end apart: 62, of which 62 were waited for; matrix products, arithmetic and copies ran while one was open for 0% of the time, Pallas kernels for 0%

commit v1 on v0

--- a/solution.py
+++ b/solution.py
@@ -139,7 +139,7 @@
     )
     outputs = (inner + carried_out + direct).reshape(tok_rows, -1)
     gated = outputs * jax.nn.silu(gate_input.astype(jnp.float32))
-    square_total = lax.psum(jnp.sum(gated * gated, axis=-1), "tp")
+    square_total = jnp.sum(lax.all_gather(jnp.sum(gated * gated, axis=-1), "tp"), axis=0)
     scaling = lax.rsqrt(square_total / (STATE_HEADS * P_SIZE) + 1e-05)
     mixer_out = (gated * scaling[:, None] * norm_gain.astype(jnp.float32)).astype(jnp.bfloat16)
     return (attention_out, mixer_out)

time: 743 us -> 742 us (level)
    psum x1 -> x0, blocking collectives: 33.4 us -> none  [local(): square_total = lax.psum(jnp.sum(gated * gated, axis=-1), 'tp')]
    all_gather x0 -> x1, blocking collectives: none -> 32.6 us  [local(): lax.all_gather(jnp.sum(gated * gated, axis=-1), 'tp')]
where the time goes in v1:
time: 742 us; the launch traced here: 739 us
  waiting for transfers between devices  477 us (64%)
  starting transfers between devices  119 us (16%)
  matrix products  52.5 us (7%)
  other arithmetic  50.5 us (7%)
  blocking collectives  32.6 us (4%)
    ppermute x62, waiting for transfers between devices, passed_along(): return lax.ppermute(block, axis, route)  477 us
    ppermute x62, starting transfers between devices, passed_along(): return lax.ppermute(block, axis, route)  119 us
    dot_general x32, matrix products, sub_step(): jnp.einsum('wlhc,cwm->wlhm', weights.astype(jnp.bfloat16), value_portion,...  33 us
    all_gather x1, blocking collectives, local(): lax.all_gather(jnp.sum(gated * gated, axis=-1), 'tp')  32.6 us
    add x31, other arithmetic, relay_step(): return (received, block_decay[..., None, None] * received + local_state)  26.1 us
    reduce_sum x32, other arithmetic, sub_step(): run_sum = run_sum * correction_factor + jnp.sum(weights, axis=-1)  16.5 us
    dot_general x32, matrix products, sub_step(): jnp.einsum('faqo,bao->aqfb', query_head_rows, key_portion, preferred_elem...  15.9 us
  transfers between devices with their start and end apart: 62, of which 62 were waited for; matrix products, arithmetic and copies ran while one was open for 0% of the time, Pallas kernels for 0%

profile of v1, /device:TPU:2, one launch (start us, length us, event | category | flops | bytes accessed | tf_op | source)
XLA Modules:
  0.0 739.3 jit_solution(33844709612663921)
XLA Ops:
  5.4 343.8 %while.55 = (s32[]{:T(128)}, bf16[2,256,128]{2,1,0:T(8,128)(2,1)S(1)}, f32[1,8,256]{2,1,0:T(8,128)S(1)}, f32[1,8,256]{2,1,0:T(8,128)S(1)}, f32[1,8,256,128]{3,2,...) while((s32[]{:T(128)}, ...), condition=%wide.region_5.6_spmd.clone, body=%wide.region_2.5_spmd.clone.sunk | while | flops 275847680 | bytes 10227923 | solution.py:94
  353.0 347.9 %while.54 = (s32[]{:T(128)}, f32[1,16,64,128]{3,2,1,0:T(8,128)}, bf16[1,16,64,128]{3,2,1,0:T(8,128)(2,1)S(1)}, f32[1,16]{1,0:T(1,128)S(1)}, f32[1,16,64,128]{3,2,1,0:T(8,128)S(1)}, /*index=5*/s32[]{:T(128)}) while((s32[]{:T(128)}, f32[1,16,64,128]{3,2,1,0:T(8,128)}, bf16[1,16,64,128]{3,2,1,0:T(8,128)(2,1)S(1)}, f32[1,16]{1,0:T(1,128)S(1)}, ...), condition=%wide.region_9.10_spmd, body=%wide.region_8.9_spmd.sunk | while | flops 524290 | bytes 2621613 | solution.py:130
  366.1 8.5 %collective-permute-done = bf16[1,16,64,128]{3,2,1,0:T(8,128)(2,1)S(1)} collective-permute-done((bf16[1,16,64,128]{3,2,1,0:T(8,128)(2,1)S(1)}, bf16[1,16,64,128]{3,2,1,0:T(8,128)(2,1)S(1)}, u32[]{:S(2)}, u32[]{:S(2)}) %collective-permute-start) | collective-permute-done | bytes 262176 | tf_op jit(solution)/shard_map/while/body/eval_jaxpr/ppermute | solution.py:17
  377.4 8.5 %collective-permute-done = bf16[1,16,64,128]{3,2,1,0:T(8,128)(2,1)S(1)} collective-permute-done((bf16[1,16,64,128]{3,2,1,0:T(8,128)(2,1)S(1)}, bf16[1,16,64,128]{3,2,1,0:T(8,128)(2,1)S(1)}, u32[]{:S(2)}, u32[]{:S(2)}) %collective-permute-start) | collective-permute-done | bytes 262176 | tf_op jit(solution)/shard_map/while/body/eval_jaxpr/ppermute | solution.py:17
  399.8 8.5 %collective-permute-done = bf16[1,16,64,128]{3,2,1,0:T(8,128)(2,1)S(1)} collective-permute-done((bf16[1,16,64,128]{3,2,1,0:T(8,128)(2,1)S(1)}, bf16[1,16,64,128]{3,2,1,0:T(8,128)(2,1)S(1)}, u32[]{:S(2)}, u32[]{:S(2)}) %collective-permute-start) | collective-permute-done | bytes 262176 | tf_op jit(solution)/shard_map/while/body/eval_jaxpr/ppermute | solution.py:17
  411.0 8.5 %collective-permute-done = bf16[1,16,64,128]{3,2,1,0:T(8,128)(2,1)S(1)} collective-permute-done((bf16[1,16,64,128]{3,2,1,0:T(8,128)(2,1)S(1)}, bf16[1,16,64,128]{3,2,1,0:T(8,128)(2,1)S(1)}, u32[]{:S(2)}, u32[]{:S(2)}) %collective-permute-start) | collective-permute-done | bytes 262176 | tf_op jit(solution)/shard_map/while/body/eval_jaxpr/ppermute | solution.py:17
  433.4 8.5 %collective-permute-done = bf16[1,16,64,128]{3,2,1,0:T(8,128)(2,1)S(1)} collective-permute-done((bf16[1,16,64,128]{3,2,1,0:T(8,128)(2,1)S(1)}, bf16[1,16,64,128]{3,2,1,0:T(8,128)(2,1)S(1)}, u32[]{:S(2)}, u32[]{:S(2)}) %collective-permute-start) | collective-permute-done | bytes 262176 | tf_op jit(solution)/shard_map/while/body/eval_jaxpr/ppermute | solution.py:17
  444.7 8.5 %collective-permute-done = bf16[1,16,64,128]{3,2,1,0:T(8,128)(2,1)S(1)} collective-permute-done((bf16[1,16,64,128]{3,2,1,0:T(8,128)(2,1)S(1)}, bf16[1,16,64,128]{3,2,1,0:T(8,128)(2,1)S(1)}, u32[]{:S(2)}, u32[]{:S(2)}) %collective-permute-start) | collective-permute-done | bytes 262176 | tf_op jit(solution)/shard_map/while/body/eval_jaxpr/ppermute | solution.py:17
  455.9 8.5 %collective-permute-done = bf16[1,16,64,128]{3,2,1,0:T(8,128)(2,1)S(1)} collective-permute-done((bf16[1,16,64,128]{3,2,1,0:T(8,128)(2,1)S(1)}, bf16[1,16,64,128]{3,2,1,0:T(8,128)(2,1)S(1)}, u32[]{:S(2)}, u32[]{:S(2)}) %collective-permute-start) | collective-permute-done | bytes 262176 | tf_op jit(solution)/shard_map/while/body/eval_jaxpr/ppermute | solution.py:17
  478.3 8.5 %collective-permute-done = bf16[1,16,64,128]{3,2,1,0:T(8,128)(2,1)S(1)} collective-permute-done((bf16[1,16,64,128]{3,2,1,0:T(8,128)(2,1)S(1)}, bf16[1,16,64,128]{3,2,1,0:T(8,128)(2,1)S(1)}, u32[]{:S(2)}, u32[]{:S(2)}) %collective-permute-start) | collective-permute-done | bytes 262176 | tf_op jit(solution)/shard_map/while/body/eval_jaxpr/ppermute | solution.py:17
  489.5 8.5 %collective-permute-done = bf16[1,16,64,128]{3,2,1,0:T(8,128)(2,1)S(1)} collective-permute-done((bf16[1,16,64,128]{3,2,1,0:T(8,128)(2,1)S(1)}, bf16[1,16,64,128]{3,2,1,0:T(8,128)(2,1)S(1)}, u32[]{:S(2)}, u32[]{:S(2)}) %collective-permute-start) | collective-permute-done | bytes 262176 | tf_op jit(solution)/shard_map/while/body/eval_jaxpr/ppermute | solution.py:17
  512.0 8.5 %collective-permute-done = bf16[1,16,64,128]{3,2,1,0:T(8,128)(2,1)S(1)} collective-permute-done((bf16[1,16,64,128]{3,2,1,0:T(8,128)(2,1)S(1)}, bf16[1,16,64,128]{3,2,1,0:T(8,128)(2,1)S(1)}, u32[]{:S(2)}, u32[]{:S(2)}) %collective-permute-start) | collective-permute-done | bytes 262176 | tf_op jit(solution)/shard_map/while/body/eval_jaxpr/ppermute | solution.py:17
  523.2 8.5 %collective-permute-done = bf16[1,16,64,128]{3,2,1,0:T(8,128)(2,1)S(1)} collective-permute-done((bf16[1,16,64,128]{3,2,1,0:T(8,128)(2,1)S(1)}, bf16[1,16,64,128]{3,2,1,0:T(8,128)(2,1)S(1)}, u32[]{:S(2)}, u32[]{:S(2)}) %collective-permute-start) | collective-permute-done | bytes 262176 | tf_op jit(solution)/shard_map/while/body/eval_jaxpr/ppermute | solution.py:17
  545.6 8.5 %collective-permute-done = bf16[1,16,64,128]{3,2,1,0:T(8,128)(2,1)S(1)} collective-permute-done((bf16[1,16,64,128]{3,2,1,0:T(8,128)(2,1)S(1)}, bf16[1,16,64,128]{3,2,1,0:T(8,128)(2,1)S(1)}, u32[]{:S(2)}, u32[]{:S(2)}) %collective-permute-start) | collective-permute-done | bytes 262176 | tf_op jit(solution)/shard_map/while/body/eval_jaxpr/ppermute | solution.py:17
  556.9 8.5 %collective-permute-done = bf16[1,16,64,128]{3,2,1,0:T(8,128)(2,1)S(1)} collective-permute-done((bf16[1,16,64,128]{3,2,1,0:T(8,128)(2,1)S(1)}, bf16[1,16,64,128]{3,2,1,0:T(8,128)(2,1)S(1)}, u32[]{:S(2)}, u32[]{:S(2)}) %collective-permute-start) | collective-permute-done | bytes 262176 | tf_op jit(solution)/shard_map/while/body/eval_jaxpr/ppermute | solution.py:17
  579.3 8.5 %collective-permute-done = bf16[1,16,64,128]{3,2,1,0:T(8,128)(2,1)S(1)} collective-permute-done((bf16[1,16,64,128]{3,2,1,0:T(8,128)(2,1)S(1)}, bf16[1,16,64,128]{3,2,1,0:T(8,128)(2,1)S(1)}, u32[]{:S(2)}, u32[]{:S(2)}) %collective-permute-start) | collective-permute-done | bytes 262176 | tf_op jit(solution)/shard_map/while/body/eval_jaxpr/ppermute | solution.py:17
  590.5 8.5 %collective-permute-done = bf16[1,16,64,128]{3,2,1,0:T(8,128)(2,1)S(1)} collective-permute-done((bf16[1,16,64,128]{3,2,1,0:T(8,128)(2,1)S(1)}, bf16[1,16,64,128]{3,2,1,0:T(8,128)(2,1)S(1)}, u32[]{:S(2)}, u32[]{:S(2)}) %collective-permute-start) | collective-permute-done | bytes 262176 | tf_op jit(solution)/shard_map/while/body/eval_jaxpr/ppermute | solution.py:17
  613.0 8.5 %collective-permute-done = bf16[1,16,64,128]{3,2,1,0:T(8,128)(2,1)S(1)} collective-permute-done((bf16[1,16,64,128]{3,2,1,0:T(8,128)(2,1)S(1)}, bf16[1,16,64,128]{3,2,1,0:T(8,128)(2,1)S(1)}, u32[]{:S(2)}, u32[]{:S(2)}) %collective-permute-start) | collective-permute-done | bytes 262176 | tf_op jit(solution)/shard_map/while/body/eval_jaxpr/ppermute | solution.py:17
  624.2 8.5 %collective-permute-done = bf16[1,16,64,128]{3,2,1,0:T(8,128)(2,1)S(1)} collective-permute-done((bf16[1,16,64,128]{3,2,1,0:T(8,128)(2,1)S(1)}, bf16[1,16,64,128]{3,2,1,0:T(8,128)(2,1)S(1)}, u32[]{:S(2)}, u32[]{:S(2)}) %collective-permute-start) | collective-permute-done | bytes 262176 | tf_op jit(solution)/shard_map/while/body/eval_jaxpr/ppermute | solution.py:17
  646.6 8.5 %collective-permute-done = bf16[1,16,64,128]{3,2,1,0:T(8,128)(2,1)S(1)} collective-permute-done((bf16[1,16,64,128]{3,2,1,0:T(8,128)(2,1)S(1)}, bf16[1,16,64,128]{3,2,1,0:T(8,128)(2,1)S(1)}, u32[]{:S(2)}, u32[]{:S(2)}) %collective-permute-start) | collective-permute-done | bytes 262176 | tf_op jit(solution)/shard_map/while/body/eval_jaxpr/ppermute | solution.py:17
  657.8 8.5 %collective-permute-done = bf16[1,16,64,128]{3,2,1,0:T(8,128)(2,1)S(1)} collective-permute-done((bf16[1,16,64,128]{3,2,1,0:T(8,128)(2,1)S(1)}, bf16[1,16,64,128]{3,2,1,0:T(8,128)(2,1)S(1)}, u32[]{:S(2)}, u32[]{:S(2)}) %collective-permute-start) | collective-permute-done | bytes 262176 | tf_op jit(solution)/shard_map/while/body/eval_jaxpr/ppermute | solution.py:17
  680.3 8.5 %collective-permute-done = bf16[1,16,64,128]{3,2,1,0:T(8,128)(2,1)S(1)} collective-permute-done((bf16[1,16,64,128]{3,2,1,0:T(8,128)(2,1)S(1)}, bf16[1,16,64,128]{3,2,1,0:T(8,128)(2,1)S(1)}, u32[]{:S(2)}, u32[]{:S(2)}) %collective-permute-start) | collective-permute-done | bytes 262176 | tf_op jit(solution)/shard_map/while/body/eval_jaxpr/ppermute | solution.py:17
  691.5 8.5 %collective-permute-done = bf16[1,16,64,128]{3,2,1,0:T(8,128)(2,1)S(1)} collective-permute-done((bf16[1,16,64,128]{3,2,1,0:T(8,128)(2,1)S(1)}, bf16[1,16,64,128]{3,2,1,0:T(8,128)(2,1)S(1)}, u32[]{:S(2)}, u32[]{:S(2)}) %collective-permute-start) | collective-permute-done | bytes 262176 | tf_op jit(solution)/shard_map/while/body/eval_jaxpr/ppermute | solution.py:17
  705.6 32.6 %all-gather.1 = f32[8,1,256]{2,1,0:T(1,128)S(1)} all-gather(f32[1,1,256]{2,1,0:T(1,128)S(1)} %bitcast.215), channel_id=2, replica_groups=mesh['ctx'=32,'tp'=8] {'tp'}, dimensions={0}, use_global_device_ids=true | all-gather | bytes 9216 | tf_op jit(solution)/shard_map/all_gather | solution.py:142
  (474 shorter events, 524.9 us)
Async XLA Ops:
  353.0 10.4 %collective-permute-start = (bf16[1,16,64,128]{3,2,1,0:T(8,128)(2,1)S(1)}, bf16[1,16,64,128]{3,2,1,0:T(8,128)(2,1)S(1)}, u32[]{:S(2)}, u32[]{:S(2)}) collective-permute-start(bf16[1,16,64,128]{3,2,1,0:T(8,128)(2,1)S(1)} %get-tuple-element.479), channel_id=1, source_target_pairs={{0,8},{8,16},{16,24},{24,32},{32,40},{40,48},{48,56},{56,64},{64,7... | collective-permute-start | bytes 786440 | tf_op jit(solution)/shard_map/while/body/eval_jaxpr/ppermute | solution.py:17
  364.2 10.4 %collective-permute-start = (bf16[1,16,64,128]{3,2,1,0:T(8,128)(2,1)S(1)}, bf16[1,16,64,128]{3,2,1,0:T(8,128)(2,1)S(1)}, u32[]{:S(2)}, u32[]{:S(2)}) collective-permute-start(bf16[1,16,64,128]{3,2,1,0:T(8,128)(2,1)S(1)} %get-tuple-element.479), channel_id=1, source_target_pairs={{0,8},{8,16},{16,24},{24,32},{32,40},{40,48},{48,56},{56,64},{64,7... | collective-permute-start | bytes 786440 | tf_op jit(solution)/shard_map/while/body/eval_jaxpr/ppermute | solution.py:17
  375.4 10.4 %collective-permute-start = (bf16[1,16,64,128]{3,2,1,0:T(8,128)(2,1)S(1)}, bf16[1,16,64,128]{3,2,1,0:T(8,128)(2,1)S(1)}, u32[]{:S(2)}, u32[]{:S(2)}) collective-permute-start(bf16[1,16,64,128]{3,2,1,0:T(8,128)(2,1)S(1)} %get-tuple-element.479), channel_id=1, source_target_pairs={{0,8},{8,16},{16,24},{24,32},{32,40},{40,48},{48,56},{56,64},{64,7... | collective-permute-start | bytes 786440 | tf_op jit(solution)/shard_map/while/body/eval_jaxpr/ppermute | solution.py:17
  386.7 10.4 %collective-permute-start = (bf16[1,16,64,128]{3,2,1,0:T(8,128)(2,1)S(1)}, bf16[1,16,64,128]{3,2,1,0:T(8,128)(2,1)S(1)}, u32[]{:S(2)}, u32[]{:S(2)}) collective-permute-start(bf16[1,16,64,128]{3,2,1,0:T(8,128)(2,1)S(1)} %get-tuple-element.479), channel_id=1, source_target_pairs={{0,8},{8,16},{16,24},{24,32},{32,40},{40,48},{48,56},{56,64},{64,7... | collective-permute-start | bytes 786440 | tf_op jit(solution)/shard_map/while/body/eval_jaxpr/ppermute | solution.py:17
  397.9 10.4 %collective-permute-start = (bf16[1,16,64,128]{3,2,1,0:T(8,128)(2,1)S(1)}, bf16[1,16,64,128]{3,2,1,0:T(8,128)(2,1)S(1)}, u32[]{:S(2)}, u32[]{:S(2)}) collective-permute-start(bf16[1,16,64,128]{3,2,1,0:T(8,128)(2,1)S(1)} %get-tuple-element.479), channel_id=1, source_target_pairs={{0,8},{8,16},{16,24},{24,32},{32,40},{40,48},{48,56},{56,64},{64,7... | collective-permute-start | bytes 786440 | tf_op jit(solution)/shard_map/while/body/eval_jaxpr/ppermute | solution.py:17
  409.1 10.4 %collective-permute-start = (bf16[1,16,64,128]{3,2,1,0:T(8,128)(2,1)S(1)}, bf16[1,16,64,128]{3,2,1,0:T(8,128)(2,1)S(1)}, u32[]{:S(2)}, u32[]{:S(2)}) collective-permute-start(bf16[1,16,64,128]{3,2,1,0:T(8,128)(2,1)S(1)} %get-tuple-element.479), channel_id=1, source_target_pairs={{0,8},{8,16},{16,24},{24,32},{32,40},{40,48},{48,56},{56,64},{64,7... | collective-permute-start | bytes 786440 | tf_op jit(solution)/shard_map/while/body/eval_jaxpr/ppermute | solution.py:17
  420.3 10.4 %collective-permute-start = (bf16[1,16,64,128]{3,2,1,0:T(8,128)(2,1)S(1)}, bf16[1,16,64,128]{3,2,1,0:T(8,128)(2,1)S(1)}, u32[]{:S(2)}, u32[]{:S(2)}) collective-permute-start(bf16[1,16,64,128]{3,2,1,0:T(8,128)(2,1)S(1)} %get-tuple-element.479), channel_id=1, source_target_pairs={{0,8},{8,16},{16,24},{24,32},{32,40},{40,48},{48,56},{56,64},{64,7... | collective-permute-start | bytes 786440 | tf_op jit(solution)/shard_map/while/body/eval_jaxpr/ppermute | solution.py:17
  431.5 10.4 %collective-permute-start = (bf16[1,16,64,128]{3,2,1,0:T(8,128)(2,1)S(1)}, bf16[1,16,64,128]{3,2,1,0:T(8,128)(2,1)S(1)}, u32[]{:S(2)}, u32[]{:S(2)}) collective-permute-start(bf16[1,16,64,128]{3,2,1,0:T(8,128)(2,1)S(1)} %get-tuple-element.479), channel_id=1, source_target_pairs={{0,8},{8,16},{16,24},{24,32},{32,40},{40,48},{48,56},{56,64},{64,7... | collective-permute-start | bytes 786440 | tf_op jit(solution)/shard_map/while/body/eval_jaxpr/ppermute | solution.py:17
  442.8 10.4 %collective-permute-start = (bf16[1,16,64,128]{3,2,1,0:T(8,128)(2,1)S(1)}, bf16[1,16,64,128]{3,2,1,0:T(8,128)(2,1)S(1)}, u32[]{:S(2)}, u32[]{:S(2)}) collective-permute-start(bf16[1,16,64,128]{3,2,1,0:T(8,128)(2,1)S(1)} %get-tuple-element.479), channel_id=1, source_target_pairs={{0,8},{8,16},{16,24},{24,32},{32,40},{40,48},{48,56},{56,64},{64,7... | collective-permute-start | bytes 786440 | tf_op jit(solution)/shard_map/while/body/eval_jaxpr/ppermute | solution.py:17
  454.0 10.4 %collective-permute-start = (bf16[1,16,64,128]{3,2,1,0:T(8,128)(2,1)S(1)}, bf16[1,16,64,128]{3,2,1,0:T(8,128)(2,1)S(1)}, u32[]{:S(2)}, u32[]{:S(2)}) collective-permute-start(bf16[1,16,64,128]{3,2,1,0:T(8,128)(2,1)S(1)} %get-tuple-element.479), channel_id=1, source_target_pairs={{0,8},{8,16},{16,24},{24,32},{32,40},{40,48},{48,56},{56,64},{64,7... | collective-permute-start | bytes 786440 | tf_op jit(solution)/shard_map/while/body/eval_jaxpr/ppermute | solution.py:17
  465.2 10.4 %collective-permute-start = (bf16[1,16,64,128]{3,2,1,0:T(8,128)(2,1)S(1)}, bf16[1,16,64,128]{3,2,1,0:T(8,128)(2,1)S(1)}, u32[]{:S(2)}, u32[]{:S(2)}) collective-permute-start(bf16[1,16,64,128]{3,2,1,0:T(8,128)(2,1)S(1)} %get-tuple-element.479), channel_id=1, source_target_pairs={{0,8},{8,16},{16,24},{24,32},{32,40},{40,48},{48,56},{56,64},{64,7... | collective-permute-start | bytes 786440 | tf_op jit(solution)/shard_map/while/body/eval_jaxpr/ppermute | solution.py:17
  476.4 10.4 %collective-permute-start = (bf16[1,16,64,128]{3,2,1,0:T(8,128)(2,1)S(1)}, bf16[1,16,64,128]{3,2,1,0:T(8,128)(2,1)S(1)}, u32[]{:S(2)}, u32[]{:S(2)}) collective-permute-start(bf16[1,16,64,128]{3,2,1,0:T(8,128)(2,1)S(1)} %get-tuple-element.479), channel_id=1, source_target_pairs={{0,8},{8,16},{16,24},{24,32},{32,40},{40,48},{48,56},{56,64},{64,7... | collective-permute-start | bytes 786440 | tf_op jit(solution)/shard_map/while/body/eval_jaxpr/ppermute | solution.py:17
  487.6 10.4 %collective-permute-start = (bf16[1,16,64,128]{3,2,1,0:T(8,128)(2,1)S(1)}, bf16[1,16,64,128]{3,2,1,0:T(8,128)(2,1)S(1)}, u32[]{:S(2)}, u32[]{:S(2)}) collective-permute-start(bf16[1,16,64,128]{3,2,1,0:T(8,128)(2,1)S(1)} %get-tuple-element.479), channel_id=1, source_target_pairs={{0,8},{8,16},{16,24},{24,32},{32,40},{40,48},{48,56},{56,64},{64,7... | collective-permute-start | bytes 786440 | tf_op jit(solution)/shard_map/while/body/eval_jaxpr/ppermute | solution.py:17
  498.8 10.4 %collective-permute-start = (bf16[1,16,64,128]{3,2,1,0:T(8,128)(2,1)S(1)}, bf16[1,16,64,128]{3,2,1,0:T(8,128)(2,1)S(1)}, u32[]{:S(2)}, u32[]{:S(2)}) collective-permute-start(bf16[1,16,64,128]{3,2,1,0:T(8,128)(2,1)S(1)} %get-tuple-element.479), channel_id=1, source_target_pairs={{0,8},{8,16},{16,24},{24,32},{32,40},{40,48},{48,56},{56,64},{64,7... | collective-permute-start | bytes 786440 | tf_op jit(solution)/shard_map/while/body/eval_jaxpr/ppermute | solution.py:17
  510.1 10.4 %collective-permute-start = (bf16[1,16,64,128]{3,2,1,0:T(8,128)(2,1)S(1)}, bf16[1,16,64,128]{3,2,1,0:T(8,128)(2,1)S(1)}, u32[]{:S(2)}, u32[]{:S(2)}) collective-permute-start(bf16[1,16,64,128]{3,2,1,0:T(8,128)(2,1)S(1)} %get-tuple-element.479), channel_id=1, source_target_pairs={{0,8},{8,16},{16,24},{24,32},{32,40},{40,48},{48,56},{56,64},{64,7... | collective-permute-start | bytes 786440 | tf_op jit(solution)/shard_map/while/body/eval_jaxpr/ppermute | solution.py:17
  521.3 10.4 %collective-permute-start = (bf16[1,16,64,128]{3,2,1,0:T(8,128)(2,1)S(1)}, bf16[1,16,64,128]{3,2,1,0:T(8,128)(2,1)S(1)}, u32[]{:S(2)}, u32[]{:S(2)}) collective-permute-start(bf16[1,16,64,128]{3,2,1,0:T(8,128)(2,1)S(1)} %get-tuple-element.479), channel_id=1, source_target_pairs={{0,8},{8,16},{16,24},{24,32},{32,40},{40,48},{48,56},{56,64},{64,7... | collective-permute-start | bytes 786440 | tf_op jit(solution)/shard_map/while/body/eval_jaxpr/ppermute | solution.py:17
  532.5 10.4 %collective-permute-start = (bf16[1,16,64,128]{3,2,1,0:T(8,128)(2,1)S(1)}, bf16[1,16,64,128]{3,2,1,0:T(8,128)(2,1)S(1)}, u32[]{:S(2)}, u32[]{:S(2)}) collective-permute-start(bf16[1,16,64,128]{3,2,1,0:T(8,128)(2,1)S(1)} %get-tuple-element.479), channel_id=1, source_target_pairs={{0,8},{8,16},{16,24},{24,32},{32,40},{40,48},{48,56},{56,64},{64,7... | collective-permute-start | bytes 786440 | tf_op jit(solution)/shard_map/while/body/eval_jaxpr/ppermute | solution.py:17
  554.9 10.4 %collective-permute-start = (bf16[1,16,64,128]{3,2,1,0:T(8,128)(2,1)S(1)}, bf16[1,16,64,128]{3,2,1,0:T(8,128)(2,1)S(1)}, u32[]{:S(2)}, u32[]{:S(2)}) collective-permute-start(bf16[1,16,64,128]{3,2,1,0:T(8,128)(2,1)S(1)} %get-tuple-element.479), channel_id=1, source_target_pairs={{0,8},{8,16},{16,24},{24,32},{32,40},{40,48},{48,56},{56,64},{64,7... | collective-permute-start | bytes 786440 | tf_op jit(solution)/shard_map/while/body/eval_jaxpr/ppermute | solution.py:17
  588.6 10.4 %collective-permute-start = (bf16[1,16,64,128]{3,2,1,0:T(8,128)(2,1)S(1)}, bf16[1,16,64,128]{3,2,1,0:T(8,128)(2,1)S(1)}, u32[]{:S(2)}, u32[]{:S(2)}) collective-permute-start(bf16[1,16,64,128]{3,2,1,0:T(8,128)(2,1)S(1)} %get-tuple-element.479), channel_id=1, source_target_pairs={{0,8},{8,16},{16,24},{24,32},{32,40},{40,48},{48,56},{56,64},{64,7... | collective-permute-start | bytes 786440 | tf_op jit(solution)/shard_map/while/body/eval_jaxpr/ppermute | solution.py:17
  622.3 10.4 %collective-permute-start = (bf16[1,16,64,128]{3,2,1,0:T(8,128)(2,1)S(1)}, bf16[1,16,64,128]{3,2,1,0:T(8,128)(2,1)S(1)}, u32[]{:S(2)}, u32[]{:S(2)}) collective-permute-start(bf16[1,16,64,128]{3,2,1,0:T(8,128)(2,1)S(1)} %get-tuple-element.479), channel_id=1, source_target_pairs={{0,8},{8,16},{16,24},{24,32},{32,40},{40,48},{48,56},{56,64},{64,7... | collective-permute-start | bytes 786440 | tf_op jit(solution)/shard_map/while/body/eval_jaxpr/ppermute | solution.py:17
  655.9 10.4 %collective-permute-start = (bf16[1,16,64,128]{3,2,1,0:T(8,128)(2,1)S(1)}, bf16[1,16,64,128]{3,2,1,0:T(8,128)(2,1)S(1)}, u32[]{:S(2)}, u32[]{:S(2)}) collective-permute-start(bf16[1,16,64,128]{3,2,1,0:T(8,128)(2,1)S(1)} %get-tuple-element.479), channel_id=1, source_target_pairs={{0,8},{8,16},{16,24},{24,32},{32,40},{40,48},{48,56},{56,64},{64,7... | collective-permute-start | bytes 786440 | tf_op jit(solution)/shard_map/while/body/eval_jaxpr/ppermute | solution.py:17
  667.1 10.4 %collective-permute-start = (bf16[1,16,64,128]{3,2,1,0:T(8,128)(2,1)S(1)}, bf16[1,16,64,128]{3,2,1,0:T(8,128)(2,1)S(1)}, u32[]{:S(2)}, u32[]{:S(2)}) collective-permute-start(bf16[1,16,64,128]{3,2,1,0:T(8,128)(2,1)S(1)} %get-tuple-element.479), channel_id=1, source_target_pairs={{0,8},{8,16},{16,24},{24,32},{32,40},{40,48},{48,56},{56,64},{64,7... | collective-permute-start | bytes 786440 | tf_op jit(solution)/shard_map/while/body/eval_jaxpr/ppermute | solution.py:17
  678.4 10.4 %collective-permute-start = (bf16[1,16,64,128]{3,2,1,0:T(8,128)(2,1)S(1)}, bf16[1,16,64,128]{3,2,1,0:T(8,128)(2,1)S(1)}, u32[]{:S(2)}, u32[]{:S(2)}) collective-permute-start(bf16[1,16,64,128]{3,2,1,0:T(8,128)(2,1)S(1)} %get-tuple-element.479), channel_id=1, source_target_pairs={{0,8},{8,16},{16,24},{24,32},{32,40},{40,48},{48,56},{56,64},{64,7... | collective-permute-start | bytes 786440 | tf_op jit(solution)/shard_map/while/body/eval_jaxpr/ppermute | solution.py:17
  689.6 10.4 %collective-permute-start = (bf16[1,16,64,128]{3,2,1,0:T(8,128)(2,1)S(1)}, bf16[1,16,64,128]{3,2,1,0:T(8,128)(2,1)S(1)}, u32[]{:S(2)}, u32[]{:S(2)}) collective-permute-start(bf16[1,16,64,128]{3,2,1,0:T(8,128)(2,1)S(1)} %get-tuple-element.479), channel_id=1, source_target_pairs={{0,8},{8,16},{16,24},{24,32},{32,40},{40,48},{48,56},{56,64},{64,7... | collective-permute-start | bytes 786440 | tf_op jit(solution)/shard_map/while/body/eval_jaxpr/ppermute | solution.py:17
  (48 other events, 1066.5 us)
